TPU v7x, 128 devices: a whole 4x4x4 slice. The times are simulated.
128 devices in a mesh: ctx: 16 (over y_lo, z, core), head: 8 (over x, y_hi).
Axes of the slice: x: 4, y: 4 (y_hi: 2, y_lo: 2; y = y_hi * 2 + y_lo), z: 4, core: 2. Of those that a mesh axis runs over, the one named last changes fastest.
Arguments:
- hidden_in: bfloat16 [4096, 8192], P('ctx', 'head'), may hold values from -90 to 90
- query_rows: bfloat16 [4096, 8192], P('ctx', 'head'), may hold values from -5 to 5
- key_rows: bfloat16 [4096, 1024], P('ctx', 'head'), may hold values from -5 to 5
- value_rows: bfloat16 [4096, 1024], P('ctx', 'head'), may hold values from -6 to 6
- out_weight: bfloat16 [8192, 8192], P('head'), may hold values from -0.0625 to 0.0625
- grad_out: bfloat16 [4096, 8192], P('ctx', 'head'), may hold values from -6 to 6
- answer_mask: int32 [4096], P('ctx'), may hold values 0 or 1
Outputs:
- grad_query: bfloat16 [4096, 8192], P('ctx', 'head')
- grad_key: bfloat16 [4096, 1024], P('ctx', 'head')
- grad_value: bfloat16 [4096, 1024], P('ctx', 'head')
- fisher_q: float32 [16, 64], P('ctx', 'head')
- fisher_o: float32 [16, 64], P('ctx', 'head')
All inputs are finite; a program needn't handle non-finite values. No bound on the sum of `answer_mask` on one device may be relied on, other than what follows from the above.
Results may differ from a plain program's by a relative error of at most 0.019.
Values may be sent and summed in bfloat16 or wider, within the bound.
No kernel may reach another device: no remote copies, remote signals or barrier semaphores. Data moves between devices by JAX's collectives and lax.ppermute only.
A program may use at most 128 MiB of HBM per device.

v0:
```python
import math
import jax
import jax.numpy as jnp
from jax import lax
from jax.sharding import PartitionSpec as P

D = 8192
HEADS = 64
KVH = 8
HD = 128
NEGATIVE = -1e30
EPSILON = 1e-06


def block_scores(query_group, key_block, scaling, row_pos, col_pos):
    scores = (
        jnp.einsum("tgd,kd->tgk", query_group, key_block, preferred_element_type=jnp.float32)
        * scaling
    )
    return jnp.where(row_pos[:, None, None] >= col_pos[None, None, :], scores, NEGATIVE)


def head_squares(left_side, right_side, head_dim):
    product = lax.dot_general(
        left_side, right_side, (((0,), (0,)), ((), ())), preferred_element_type=jnp.float32
    )
    shaped = (product * product).reshape(
        product.shape[0], right_side.shape[1] // head_dim, head_dim
    )
    return jnp.sum(shaped, axis=(0, 2))


def gram_pair_squares(left_gram, right_side, head_dim):
    rows = right_side.shape[0]
    right_heads = right_side.reshape(rows, right_side.shape[1] // head_dim, head_dim)
    right_gram = jnp.einsum(
        "ihd,jhd->hij", right_heads, right_heads, preferred_element_type=jnp.float32
    )
    return jnp.sum(right_gram * left_gram[None], axis=(1, 2))


def gram_squares(left_side, right_side, head_dim):
    left_gram = lax.dot_general(
        left_side, left_side, (((1,), (1,)), ((), ())), preferred_element_type=jnp.float32
    )
    return gram_pair_squares(left_gram, right_side, head_dim)


def body(hidden_in, query_rows, key_rows, value_rows, out_weight, grad_out, answer_mask):
    tok_dev = query_rows.shape[0]
    head_dim = HD
    group_size = HEADS // KVH
    local_groups = key_rows.shape[1] // head_dim
    scaling = head_dim ** (-0.5)
    own_index = lax.axis_index("ctx")
    first_row = own_index * tok_dev
    loss_weight = 0.25 + answer_mask.astype(jnp.float32)
    weighted = (grad_out.astype(jnp.float32) * loss_weight[:, None]).astype(jnp.bfloat16)
    hidden_gram = lax.psum(
        lax.dot_general(
            hidden_in, hidden_in, (((1,), (1,)), ((), ())), preferred_element_type=jnp.float32
        ),
        "head",
    )
    pair_all = lax.all_gather(
        jnp.concatenate([key_rows, value_rows], axis=1), "ctx", axis=0, tiled=True
    )
    kv_width = key_rows.shape[1]
    keys_all, values_all = (pair_all[:, :kv_width], pair_all[:, kv_width:])
    tokens = keys_all.shape[0]
    block_rows = math.gcd(512, tokens)

    def fetch(table, block_number):
        return lax.dynamic_slice_in_dim(table, block_number * block_rows, block_rows, 0)

    def column_pos(block_number):
        return block_number * block_rows + jnp.arange(block_rows, dtype=jnp.int32)

    buffer = jnp.zeros((tokens, 2 * local_groups * head_dim), jnp.float32)
    rows = query_rows.shape[0]
    row_pos = first_row + jnp.arange(rows, dtype=jnp.int32)
    needed = (first_row + rows - 1) // block_rows + 1
    query_heads = query_rows.reshape(rows, local_groups, group_size, head_dim)
    log_totals = []
    shared_head = 0
    query_group = query_heads[:, shared_head]

    def stats_step(block_number, carried):
        running_max, running_sum = carried
        key_block = fetch(keys_all, block_number)
        scores = block_scores(query_group, key_block, scaling, row_pos, column_pos(block_number))
        new_max = jnp.maximum(running_max, jnp.max(scores, axis=-1))
        running_sum = running_sum * jnp.exp(running_max - new_max) + jnp.sum(
            jnp.exp(scores - new_max[..., None]), axis=-1
        )
        return (new_max, running_sum)

    start_max = jnp.full((rows, group_size), NEGATIVE, jnp.float32)
    start_sum = jnp.zeros((rows, group_size), jnp.float32)
    running_max, running_sum = lax.fori_loop(0, needed, stats_step, (start_max, start_sum))
    log_total = running_max + jnp.log(running_sum)

    def value_step(block_number, accumulated):
        key_block = fetch(keys_all, block_number)
        value_block = fetch(values_all, block_number)
        scores = block_scores(query_group, key_block, scaling, row_pos, column_pos(block_number))
        rounded = jnp.exp(scores - log_total[..., None]).astype(jnp.bfloat16)
        return accumulated + jnp.einsum(
            "tgk,kd->tgd", rounded, value_block, preferred_element_type=jnp.float32
        )

    accumulated = lax.fori_loop(
        0, needed, value_step, jnp.zeros((rows, group_size, head_dim), jnp.float32)
    )
    log_totals.append(log_total)
    attended_list = [accumulated.astype(jnp.bfloat16)]
    attended_part = jnp.stack(attended_list, axis=1).reshape(
        rows, local_groups * group_size * head_dim
    )
    log_totals, attended = (log_totals, attended_part)
    piece_part = lax.all_gather(weighted, "head", axis=1, tiled=True)
    grad_sum = lax.dot_general(
        piece_part, out_weight, (((1,), (1,)), ((), ())), preferred_element_type=jnp.float32
    )
    grad_sum, squares_out = (grad_sum, gram_squares(piece_part, attended, head_dim))
    grad_attended, squares_out = (grad_sum.astype(jnp.bfloat16), squares_out)
    backward_buffer = buffer
    rows = query_rows.shape[0]
    backward_row_pos = first_row + jnp.arange(rows, dtype=jnp.int32)
    needed = (first_row + rows - 1) // block_rows + 1
    query_heads = query_rows.reshape(rows, local_groups, group_size, head_dim)
    grad_heads = grad_attended.reshape(rows, local_groups, group_size, head_dim)
    attended_heads = attended.reshape(rows, local_groups, group_size, head_dim)
    shared_head = 0
    backward_query_group = query_heads[:, shared_head]
    grad_group = grad_heads[:, shared_head]
    backward_log_total = log_totals[shared_head]
    row_dot = jnp.sum(
        grad_group.astype(jnp.float32) * attended_heads[:, shared_head].astype(jnp.float32), axis=-1
    )
    key_column = jnp.int32(shared_head * head_dim)
    value_column = jnp.int32((local_groups + shared_head) * head_dim)

    def back_step(block_number, carried):
        query_sum, buffer_now = carried
        key_block = fetch(keys_all, block_number)
        value_block = fetch(values_all, block_number)
        scores = block_scores(
            backward_query_group, key_block, scaling, backward_row_pos, column_pos(block_number)
        )
        softmax = jnp.exp(scores - backward_log_total[..., None])
        rounded = softmax.astype(jnp.bfloat16)
        grad_prob = jnp.einsum(
            "tgd,kd->tgk", grad_group, value_block, preferred_element_type=jnp.float32
        )
        grad_score = (softmax * (grad_prob - row_dot[..., None]) * scaling).astype(jnp.bfloat16)
        query_sum = query_sum + jnp.einsum(
            "tgk,kd->tgd", grad_score, key_block, preferred_element_type=jnp.float32
        )
        key_part = jnp.einsum(
            "tgk,tgd->kd", grad_score, backward_query_group, preferred_element_type=jnp.float32
        )
        value_part = jnp.einsum(
            "tgk,tgd->kd", rounded, grad_group, preferred_element_type=jnp.float32
        )
        row_start = (block_number * block_rows).astype(jnp.int32)
        old_key = lax.dynamic_slice(buffer_now, (row_start, key_column), (block_rows, head_dim))
        buffer_now = lax.dynamic_update_slice(
            buffer_now, old_key + key_part, (row_start, key_column)
        )
        old_value = lax.dynamic_slice(buffer_now, (row_start, value_column), (block_rows, head_dim))
        buffer_now = lax.dynamic_update_slice(
            buffer_now, old_value + value_part, (row_start, value_column)
        )
        return (query_sum, buffer_now)

    start_query = jnp.zeros((rows, group_size, head_dim), jnp.float32)
    query_sum, backward_buffer = lax.fori_loop(0, needed, back_step, (start_query, backward_buffer))
    query_grads = [query_sum.astype(jnp.bfloat16)]
    grad_query_part = jnp.stack(query_grads, axis=1).reshape(
        rows, local_groups * group_size * head_dim
    )
    key_sums = lax.psum_scatter(
        backward_buffer.astype(jnp.bfloat16), "ctx", scatter_dimension=0, tiled=True
    ).astype(jnp.float32)
    grad_key = key_sums[:, : local_groups * head_dim].astype(jnp.bfloat16)
    grad_value = key_sums[:, local_groups * head_dim :].astype(jnp.bfloat16)
    squares_query = gram_pair_squares(hidden_gram, grad_query_part, head_dim)
    normal_size = D * head_dim * tok_dev
    fisher_q = jnp.log(squares_query / normal_size + EPSILON).reshape(1, -1)
    fisher_o = jnp.log(squares_out / normal_size + EPSILON).reshape(1, -1)
    return (grad_query_part, grad_key, grad_value, fisher_q, fisher_o)


def solution(mesh):
    return jax.shard_map(
        body,
        mesh=mesh,
        in_specs=(
            P("ctx", "head"),
            P("ctx", "head"),
            P("ctx", "head"),
            P("ctx", "head"),
            P("head", None),
            P("ctx", "head"),
            P("ctx"),
        ),
        out_specs=(
            P("ctx", "head"),
            P("ctx", "head"),
            P("ctx", "head"),
            P("ctx", "head"),
            P("ctx", "head"),
        ),
        check_vma=False,
    )
```

profile of v0, /device:TPU:0, one launch (start us, length us, event | category | flops | bytes accessed | tf_op | source)
XLA Modules:
  0.0 287.8 jit_solution(4906694200121494240)
XLA Ops:
  7.2 0.0 all-gather.3.cloned.1.call-start
  7.2 1.6 pad_maximum_fusion
  8.8 0.0 all-gather.3.cloned.1.call-update
  8.8 0.0 all-gather.5.cloned.1.call-start
  8.9 0.7 convert_add_fusion
  9.6 2.0 multiply_convert_fusion
  11.6 0.0 all-gather.5.cloned.1.call-update
  11.6 0.0 all-reduce.2.cloned.1.call-start
  11.6 1.0 fusion.64
  12.7 0.0 all-reduce.2.cloned.1.call-update
  12.7 0.0 reduce-scatter.2.cloned.1.call-start
  12.8 1.2 copy.18
  14.0 0.3 copy.22
  14.3 1.1 copy.21
  15.4 31.1 %all-gather.3.cloned.1.call-done = bf16[4096,256]{1,0:T(8,128)(2,1)} async-done(((bf16[256,256]{1,0:T(8,128)(2,1)}), bf16[4096,256]{1,0:T(8,128)(2,1)}) %all-gather.3.cloned.1.call-update) | async-done | bytes 2097168 | tf_op jit(solution)/shard_map/all_gather | solution.py:65
  46.4 2.7 fusion.62
  49.2 1.9 while.37
  49.2 0.1 broadcast_compare_fusion.6
  49.3 0.8 fusion.100
  50.1 0.9 exponential_reduce_fusion.2
  51.1 0.1 broadcast.137.clone
  51.1 3.0 %while.38 = (s32[]{:T(128)}, f32[256,8,128]{2,0,1:T(8,128)S(1)}, s32[]{:T(128)}, bf16[4096,128]{1,0:T(8,128)(2,1)S(1)}, bf16[256,8,128]{2,1,0:T(8,128)(2,1)}, /*...) while((s32[]{:T(128)}, f32[256,8,128]{2,0,1:T(8,128)S(1)}, ...), condition=%wide.region_5.6_spmd.clone, body=%wide.region_4.5_spmd.clone.sunk | while | flops 541459200 | bytes 3161259 | solution.py:112
  51.2 0.1 broadcast_compare_fusion.7
  51.3 2.8 fusion.104
  54.1 65.9 %all-gather.5.cloned.1.call-done = bf16[256,8192]{1,0:T(8,128)(2,1)} async-done(((bf16[256,1024]{1,0:T(8,128)(2,1)}), bf16[256,8192]{1,0:T(8,128)(2,1)}) %all-gather.5.cloned.1.call-update) | async-done | bytes 4194320 | tf_op jit(solution)/shard_map/all_gather | solution.py:121
  120.1 12.4 %fusion.59 = bf16[32,8,8,128]{3,2,1,0:T(8,128)(2,1)} fusion(bf16[256,8192]{1,0:T(8,128)(2,1)} %all-gather.5.cloned.1.call-done, bf16[1024,8192]{1,0:T(8,128)(2,1)} %param.17), kind=kOutput, calls=%fused_computation.65 | convolution fusion | flops 4295229440 | bytes 21495808 | tf_op jit(solution)/shard_map/dot_general | solution.py:122
  132.4 1.9 copy.36
  134.4 1.4 multiply_reduce_fusion.2
  135.8 0.1 broadcast.137
  135.8 2.2 broadcast_in_dim.50
  138.1 9.5 %while.39 = (s32[]{:T(128)}, f32[256,8,128]{2,0,1:T(8,128)S(1)}, f32[4096,256]{1,0:T(8,128)}, s32[]{:T(128)}, bf16[4096,128]{1,0:T(8,128)(2,1)S(1)}, /*index=5*/...) while((s32[]{:T(128)}, f32[256,8,128]{2,0,1:T(8,128)S(1)}, ...), condition=%wide.region_8.9_spmd.clone, body=%wide.region_7.8_spmd.clone.sunk | while | flops 1354236672 | bytes 27031796 | solution.py:178
  138.1 0.1 broadcast_compare_fusion.8
  138.2 0.7 fusion.115
  139.0 0.2 copy-done.3
  139.1 2.4 fusion.116
  141.5 0.9 convolution_add_fusion.2
  142.5 2.4 fusion.117
  144.9 2.7 fusion.118
  147.6 3.8 %convert_element_type.47 = bf16[4096,256]{1,0:T(8,128)(2,1)} convert(f32[4096,256]{1,0:T(8,128)} %get-tuple-element.150) | non-fusion elementwise | flops 1048576 | bytes 6291456 | tf_op jit(solution)/shard_map/convert_element_type | solution.py:184
  151.4 4.8 %fusion.65 = f32[256,256]{1,0:T(8,128)S(1)} fusion(bf16[256,8192]{1,0:T(8,128)(2,1)} %all-gather.5.cloned.1.call-done), kind=kOutput, calls=%fused_computation.81 | convolution fusion | flops 1073741824 | bytes 4456448 | tf_op jit(solution)/shard_map/dot_general | solution.py:43
  156.3 0.5 multiply_reduce_fusion
  156.8 47.9 %all-reduce.2.cloned.1.call-done = f32[256,256]{1,0:T(8,128)} async-done(((f32[256,256]{1,0:T(8,128)}), f32[256,256]{1,0:T(8,128)}) %all-reduce.2.cloned.1.call-update) | async-done | bytes 262160 | tf_op jit(solution)/shard_map/psum | solution.py:59
  204.7 1.5 multiply_reduce_fusion.1
  206.2 0.5 log_bitcast_fusion
  206.7 0.5 log_bitcast_fusion.1
  207.2 0.9 copy_bitcast_fusion
  208.1 71.6 %reduce-scatter.2.cloned.1.call-done = bf16[256,256]{1,0:T(8,128)(2,1)} async-done(((bf16[4096,256]{1,0:T(8,128)(2,1)}), bf16[256,256]{1,0:T(8,128)(2,1)}) %reduce-scatter.2.cloned.1.call-update) | async-done | bytes 131088 | tf_op jit(solution)/shard_map/reduce_scatter | solution.py:183
  279.7 1.5 fusion.63
  (20 shorter events, 0.1 us)
Async XLA Ops:
  7.2 4.5 %copy-start = (bf16[256,1024]{1,0:T(8,128)(2,1)S(1)}, bf16[256,1024]{1,0:T(8,128)(2,1)}, u32[]{:S(2)}) copy-start(bf16[256,1024]{1,0:T(8,128)(2,1)} %param.13) | copy-start | bytes 1572868
  7.2 39.3 %all-gather.3.cloned.1.call-start = ((), (), s32[]{:S(2)}) async-start(), calls=%async_computation.1 | async-start | bytes 2228224 | tf_op jit(solution)/shard_map/all_gather | solution.py:65
  8.8 111.3 %all-gather.5.cloned.1.call-start = ((), (), s32[]{:S(2)}) async-start(), calls=%async_computation.2 | async-start | bytes 4718592 | tf_op jit(solution)/shard_map/all_gather | solution.py:121
  11.6 193.1 %all-reduce.2.cloned.1.call-start = ((), (), s32[]{:S(2)}) async-start(), calls=%async_computation.4 | async-start | bytes 524288 | tf_op jit(solution)/shard_map/psum | solution.py:59
  12.7 267.0 %reduce-scatter.2.cloned.1.call-start = ((), (), s32[]{:S(2)}) async-start(), calls=%async_computation.3 | async-start | bytes 2228224 | tf_op jit(solution)/shard_map/reduce_scatter | solution.py:183
  54.1 80.2 %copy-start.1 = (f32[256,8,128]{2,0,1:T(8,128)}, f32[256,8,128]{2,0,1:T(8,128)S(1)}, u32[]{:S(2)}) copy-start(f32[256,8,128]{2,0,1:T(8,128)S(1)} %get-tuple-element.148) | copy-start | bytes 3145732
  138.1 1.0 copy-start.3
  151.4 4.8 %copy-start.2 = (f32[256,8,128]{2,0,1:T(8,128)S(1)}, f32[256,8,128]{2,0,1:T(8,128)}, u32[]{:S(2)}) copy-start(f32[256,8,128]{2,0,1:T(8,128)} %copy-done.1) | copy-start | bytes 3145732
Sparse Core Ops, SparseCore 0:
  9.7 36.6 all-gather.2
  48.8 71.2 all-gather.4
  122.6 82.0 all-reduce.1
  207.1 72.5 reduce-scatter.1
where the time goes:
time: 289 us; the launch traced here: 288 us
  waiting for transfers between devices  217 us (75%)
  matrix products  33 us (11%)
  between operations  13.9 us (5%)
  other arithmetic  12.7 us (4%)
  local copies, waits for them, and re-layouts  11.4 us (4%)
    reduce_scatter x1, waiting for transfers between devices, body(): lax.psum_scatter(backward_buffer.astype(jnp.bfloat16), 'ctx', scatter_dim...  71.6 us
    all_gather x1, waiting for transfers between devices, body(): piece_part = lax.all_gather(weighted, 'head', axis=1, tiled=True)  65.9 us
    psum x1, waiting for transfers between devices, body(): lax.psum(lax.dot_general(hidden_in, hidden_in, (((1,), (1,)), ((), ())),...  47.9 us
    all_gather x1, waiting for transfers between devices, body(): lax.all_gather(jnp.concatenate([key_rows, value_rows], axis=1), 'ctx', ax...  31.1 us
    dot_general x1, matrix products, body(): lax.dot_general(piece_part, out_weight, (((1,), (1,)), ((), ())), preferr...  12.4 us
  transfers between devices with their start and end apart: 4, of which 4 were waited for; matrix products, arithmetic and copies ran while one was open for 19% of the time, Pallas kernels for 0%

commit v1 on v0

--- a/solution.py
+++ b/solution.py
@@ -62,8 +62,14 @@
         ),
         "head",
     )
-    pair_all = lax.all_gather(
-        jnp.concatenate([key_rows, value_rows], axis=1), "ctx", axis=0, tiled=True
+    pair_all = jnp.concatenate(
+        lax.all_to_all(
+            jnp.stack([jnp.concatenate([key_rows, value_rows], axis=1)] * lax.axis_size("ctx")),
+            "ctx",
+            0,
+            0,
+        ),
+        axis=0,
     )
     kv_width = key_rows.shape[1]
     keys_all, values_all = (pair_all[:, :kv_width], pair_all[:, kv_width:])

time: 289 us -> 267 us (0.924)
  waiting for transfers between devices: 217 us -> 187 us
  starting transfers between devices: 0.16 us -> 6.68 us
    all_gather x1, waiting for transfers between devices: 65.9 us -> 29 us  [body(): piece_part = lax.all_gather(weighted, 'head', axis=1, tiled=True)]
    all_gather x1 -> x0, waiting for transfers between devices: 31.1 us -> none  [body(): lax.all_gather(jnp.concatenate([key_rows, value_rows], axis=1), 'ctx', ax...]
    all_to_all x0 -> x1, waiting for transfers between devices: none -> 30.7 us  [body(): lax.all_to_all(jnp.stack([jnp.concatenate([key_rows, value_rows], axis=1)...]
    reduce_scatter x1, waiting for transfers between devices: 71.6 us -> 79.8 us  [body(): lax.psum_scatter(backward_buffer.astype(jnp.bfloat16), 'ctx', scatter_dim...]
    all_to_all x0 -> x1, starting transfers between devices: none -> 6.56 us  [body(): lax.all_to_all(jnp.stack([jnp.concatenate([key_rows, value_rows], axis=1)...]
  transfers between devices with their start and end apart: 4 -> 4, of which waited for: 4 -> 4; matrix products, arithmetic and copies ran while one was open for 19% -> 20% of each run, Pallas kernels for 0% -> 0%
where the time goes in v1:
time: 267 us; the launch traced here: 265 us
  waiting for transfers between devices  187 us (70%)
  matrix products  33 us (12%)
  between operations  13.9 us (5%)
  other arithmetic  12.1 us (5%)
  local copies, waits for them, and re-layouts  11.9 us (4%)
  starting transfers between devices  6.68 us (3%)
    reduce_scatter x1, waiting for transfers between devices, body(): lax.psum_scatter(backward_buffer.astype(jnp.bfloat16), 'ctx', scatter_dim...  79.8 us
    psum x1, waiting for transfers between devices, body(): lax.psum(lax.dot_general(hidden_in, hidden_in, (((1,), (1,)), ((), ())),...  47.9 us
    all_to_all x1, waiting for transfers between devices, body(): lax.all_to_all(jnp.stack([jnp.concatenate([key_rows, value_rows], axis=1)...  30.7 us
    all_gather x1, waiting for transfers between devices, body(): piece_part = lax.all_gather(weighted, 'head', axis=1, tiled=True)  29 us
    dot_general x1, matrix products, body(): lax.dot_general(piece_part, out_weight, (((1,), (1,)), ((), ())), preferr...  12.4 us
    all_to_all x1, starting transfers between devices, body(): lax.all_to_all(jnp.stack([jnp.concatenate([key_rows, value_rows], axis=1)...  6.56 us
  transfers between devices with their start and end apart: 4, of which 4 were waited for; matrix products, arithmetic and copies ran while one was open for 20% of the time, Pallas kernels for 0%

profile of v1, /device:TPU:0, one launch (start us, length us, event | category | flops | bytes accessed | tf_op | source)
XLA Modules:
  0.0 265.1 jit_solution(16065485428916227721)
XLA Ops:
  7.2 0.0 all-gather.2.cloned.1.call-start
  7.2 0.7 convert_add_fusion
  8.0 2.0 multiply_convert_fusion
  9.9 0.0 all-gather.2.cloned.1.call-update
  10.0 0.9 pad_maximum_fusion
  10.9 1.5 stack.2
  12.5 6.6 %all-to-all-start = ((bf16[16,256,256]{2,1,0:T(8,128)(2,1)}), bf16[16,256,256]{2,1,0:T(8,128)(2,1)}, u32[]{:S(2)}, u32[]{:S(2)}) async-start(bf16[16,256,256]{2,1,0:T(8,128)(2,1)} %stack.2), calls=%async_computation | async-start | bytes 4194304 | tf_op jit(solution)/shard_map/all_to_all | solution.py:66
  19.0 0.0 all-reduce.2.cloned.1.call-start
  19.1 1.0 fusion.64
  20.1 0.0 all-reduce.2.cloned.1.call-update
  20.2 0.0 reduce-scatter.2.cloned.1.call-start
  20.2 0.2 copy.18
  20.4 0.3 copy.22
  20.7 1.1 copy.21
  21.8 30.7 %all-to-all-done = bf16[16,256,256]{2,1,0:T(8,128)(2,1)} async-done(((bf16[16,256,256]{2,1,0:T(8,128)(2,1)}), bf16[16,256,256]{2,1,0:T(8,128)(2,1)}, u32[]{:S(2)}, u32[]{:S(2)}) %all-to-all-start) | async-done | bytes 2097184 | tf_op jit(solution)/shard_map/all_to_all | solution.py:66
  52.5 2.8 %fusion.62 = (bf16[4096,128]{1,0:T(8,128)(2,1)}, bf16[4096,128]{1,0:T(8,128)(2,1)S(1)}) fusion(bf16[4096,256]{1,0:T(8,128)(2,1)} %bitcast), kind=kLoop, calls=%fused_computation.78 | loop fusion | bytes 4194304 | tf_op jit(solution)/shard_map/slice | solution.py:75
  55.3 1.9 while.37
  55.3 0.1 broadcast_compare_fusion.6
  55.5 0.8 fusion.100
  56.3 0.9 exponential_reduce_fusion.2
  57.2 0.1 broadcast.139.clone
  57.3 3.0 %while.38 = (s32[]{:T(128)}, f32[256,8,128]{2,0,1:T(8,128)S(1)}, s32[]{:T(128)}, bf16[4096,128]{1,0:T(8,128)(2,1)S(1)}, bf16[256,8,128]{2,1,0:T(8,128)(2,1)}, /*...) while((s32[]{:T(128)}, f32[256,8,128]{2,0,1:T(8,128)S(1)}, ...), condition=%wide.region_5.6_spmd.clone, body=%wide.region_4.5_spmd.clone.sunk | while | flops 541459200 | bytes 3161259 | solution.py:118
  57.3 0.1 broadcast_compare_fusion.7
  57.5 2.8 %fusion.104 = f32[256,8,128]{2,0,1:T(8,128)S(1)} fusion(f32[256,8,128]{2,0,1:T(8,128)S(1)} %get-tuple-element.530, f32[256,8]{0,1:T(8,128)S(1)} %get-tuple-element.546, pred[256,512]{1,0:T(8,128)(4,1)S(1)} %broadcast_compare_fusion.7, bf16[256,8,128]{2,1,0:T(8,128)(2,1)} %get-tuple-element.545, bf16[4096,128]{1,0:T(8,128)(2,1)} %get-tuple-element.547, ...), kind=kOutput, calls=%fused_computation.19.clone.1 | convolution fusion | flops 541327360 | bytes 3023872 | tf_op jit(solution)/shard_map/while/body/tgk,kd->tgd/dot_general | solution.py:114
  60.3 29.0 %all-gather.2.cloned.1.call-done = bf16[256,8192]{1,0:T(8,128)(2,1)} async-done(((bf16[256,1024]{1,0:T(8,128)(2,1)}), bf16[256,8192]{1,0:T(8,128)(2,1)}) %all-gather.2.cloned.1.call-update) | async-done | bytes 4194320 | tf_op jit(solution)/shard_map/all_gather | solution.py:127
  89.2 12.4 %fusion.59 = bf16[32,8,8,128]{3,2,1,0:T(8,128)(2,1)} fusion(bf16[256,8192]{1,0:T(8,128)(2,1)} %all-gather.2.cloned.1.call-done, bf16[1024,8192]{1,0:T(8,128)(2,1)} %param.17), kind=kOutput, calls=%fused_computation.65 | convolution fusion | flops 4295229440 | bytes 21495808 | tf_op jit(solution)/shard_map/dot_general | solution.py:128
  101.6 1.9 copy.36
  103.5 1.4 multiply_reduce_fusion.2
  104.9 0.1 broadcast.139
  105.0 2.2 broadcast_in_dim.50
  107.2 9.5 %while.39 = (s32[]{:T(128)}, f32[256,8,128]{2,0,1:T(8,128)S(1)}, f32[4096,256]{1,0:T(8,128)}, s32[]{:T(128)}, bf16[4096,128]{1,0:T(8,128)(2,1)S(1)}, /*index=5*/...) while((s32[]{:T(128)}, f32[256,8,128]{2,0,1:T(8,128)S(1)}, ...), condition=%wide.region_8.9_spmd.clone, body=%wide.region_7.8_spmd.clone.sunk | while | flops 1354236672 | bytes 27031796 | solution.py:184
  107.2 0.1 broadcast_compare_fusion.8
  107.4 0.7 fusion.115
  108.1 0.2 copy-done.4
  108.3 2.4 fusion.116
  110.7 0.9 convolution_add_fusion.2
  111.6 2.4 fusion.117
  114.0 2.7 %fusion.118 = f32[4096,256]{1,0:T(8,128)} fusion(f32[4096,256]{1,0:T(8,128)} %fusion.117, s32[]{:T(128)S(6)} %select_n.85, bf16[256,8,128]{2,0,1:T(8,128)(2,1)S(1)} %copy-done.4, f32[512,256,8]{1,0,2:T(8,128)S(1)} %fusion.115, f32[256,8]{0,1:T(8,128)S(1)} %get-tuple-element.589, pred[256,512]{0,1:T(8,128)(4,1)S(1)} %broadcast_compare_fusion.8), kind=kOutput, calls=%fused_computation.44.clone.1 | convolution fusion | flops 272695296 | bytes 5382148 | tf_op jit(solution)/shard_map/while/body/tgk,tgd->kd/dot_general | solution.py:169
  116.8 3.8 %convert_element_type.47 = bf16[4096,256]{1,0:T(8,128)(2,1)} convert(f32[4096,256]{1,0:T(8,128)} %get-tuple-element.150) | non-fusion elementwise | flops 1048576 | bytes 6291456 | tf_op jit(solution)/shard_map/convert_element_type | solution.py:190
  120.6 4.8 %fusion.65 = f32[256,256]{1,0:T(8,128)S(1)} fusion(bf16[256,8192]{1,0:T(8,128)(2,1)} %all-gather.2.cloned.1.call-done), kind=kOutput, calls=%fused_computation.81 | convolution fusion | flops 1073741824 | bytes 4456448 | tf_op jit(solution)/shard_map/dot_general | solution.py:43
  125.4 0.5 multiply_reduce_fusion
  126.0 47.9 %all-reduce.2.cloned.1.call-done = f32[256,256]{1,0:T(8,128)} async-done(((f32[256,256]{1,0:T(8,128)}), f32[256,256]{1,0:T(8,128)}) %all-reduce.2.cloned.1.call-update) | async-done | bytes 262160 | tf_op jit(solution)/shard_map/psum | solution.py:59
  173.8 1.5 multiply_reduce_fusion.1
  175.3 0.5 log_bitcast_fusion
  175.8 0.5 log_bitcast_fusion.1
  176.4 0.9 copy_bitcast_fusion
  177.2 79.8 %reduce-scatter.2.cloned.1.call-done = bf16[256,256]{1,0:T(8,128)(2,1)} async-done(((bf16[4096,256]{1,0:T(8,128)(2,1)}), bf16[256,256]{1,0:T(8,128)(2,1)}) %reduce-scatter.2.cloned.1.call-update) | async-done | bytes 131088 | tf_op jit(solution)/shard_map/reduce_scatter | solution.py:189
  257.0 1.5 fusion.63
  (22 shorter events, 0.1 us)
Async XLA Ops:
  7.2 11.9 %copy-start = (bf16[256,1024]{1,0:T(8,128)(2,1)S(1)}, bf16[256,1024]{1,0:T(8,128)(2,1)}, u32[]{:S(2)}) copy-start(bf16[256,1024]{1,0:T(8,128)(2,1)} %param.13) | copy-start | bytes 1572868
  7.2 82.0 %all-gather.2.cloned.1.call-start = ((), (), s32[]{:S(2)}) async-start(), calls=%async_computation.2 | async-start | bytes 4718592 | tf_op jit(solution)/shard_map/all_gather | solution.py:127
  10.0 10.2 %copy-start.3 = (bf16[256,1024]{1,0:T(8,128)(2,1)S(1)}, bf16[256,1024]{1,0:T(8,128)(2,1)}, u32[]{:S(2)}) copy-start(bf16[256,1024]{1,0:T(8,128)(2,1)} %param.14) | copy-start | bytes 1572868
  12.5 40.0 %all-to-all-start = ((bf16[16,256,256]{2,1,0:T(8,128)(2,1)}), bf16[16,256,256]{2,1,0:T(8,128)(2,1)}, u32[]{:S(2)}, u32[]{:S(2)}) async-start(bf16[16,256,256]{2,1,0:T(8,128)(2,1)} %stack.2), calls=%async_computation | async-start | bytes 4194304 | tf_op jit(solution)/shard_map/all_to_all | solution.py:66
  19.0 154.8 %all-reduce.2.cloned.1.call-start = ((), (), s32[]{:S(2)}) async-start(), calls=%async_computation.4 | async-start | bytes 524288 | tf_op jit(solution)/shard_map/psum | solution.py:59
  20.2 236.8 %reduce-scatter.2.cloned.1.call-start = ((), (), s32[]{:S(2)}) async-start(), calls=%async_computation.3 | async-start | bytes 2228224 | tf_op jit(solution)/shard_map/reduce_scatter | solution.py:189
  60.3 43.3 %copy-start.1 = (f32[256,8,128]{2,0,1:T(8,128)}, f32[256,8,128]{2,0,1:T(8,128)S(1)}, u32[]{:S(2)}) copy-start(f32[256,8,128]{2,0,1:T(8,128)S(1)} %get-tuple-element.148) | copy-start | bytes 3145732
  107.2 1.0 copy-start.4
  120.6 4.8 %copy-start.2 = (f32[256,8,128]{2,0,1:T(8,128)S(1)}, f32[256,8,128]{2,0,1:T(8,128)}, u32[]{:S(2)}) copy-start(f32[256,8,128]{2,0,1:T(8,128)} %copy-done.1) | copy-start | bytes 3145732
Sparse Core Ops, SparseCore 0:
  10.4 78.8 all-gather.1
  91.7 82.0 all-reduce.1
  176.3 80.6 reduce-scatter.1
